TPU v7x, 128 devices: a whole 4x4x4 slice. The times are simulated.
128 devices in a mesh: sta: 2 (over x_lo), gx: 16 (over x_hi, z, core), gy: 4 (over y).
Axes of the slice: x: 4 (x_hi: 2, x_lo: 2; x = x_hi * 2 + x_lo), y: 4, z: 4, core: 2. Of those that a mesh axis runs over, the one named last changes fastest.
Arguments:
- record: float32 [128, 1024], replicated, may hold values from -6 to 6
- shifts: int32 [128, 256], P(None, 'gx'), may hold values from 0 to 1022
- station_group: int32 [128], replicated, may hold values from 0 to 7
- weights: bfloat16 [128, 256, 512], P('sta', 'gy'), may hold values from -6 to 6
- psf_real: float32 [256, 256, 512], P(None, 'gx', 'gy'), may hold values from -6 to 6
- psf_imag: float32 [256, 256, 512], P(None, 'gx', 'gy'), may hold values from -6 to 6
Outputs:
- image: float32 [2, 256, 256, 512], P('sta', 'gx', 'gy')
All inputs are finite; a program needn't handle non-finite values.
Results may differ from a plain program's by a relative error of at most 0.0029.
Values may be sent and summed in bfloat16 or wider, within the bound.
No kernel may reach another device: no remote copies, remote signals or barrier semaphores. Data moves between devices by JAX's collectives and lax.ppermute only.
A program may use at most 128 MiB of HBM per device.

v0:
```python
import math
import jax
import jax.numpy as jnp
from jax import lax
from jax.sharding import PartitionSpec as P

T_DEV = 1
NZ = 256
NX = 256
GROUPS = 8
NOISE_POWER = 0.25
HIGHEST = lax.Precision.HIGHEST


def station_counts(station_group):
    labels = jnp.arange(GROUPS, dtype=jnp.int32)
    onehot = (station_group[:, None] == labels[None, :]).astype(jnp.float32)
    totals = jnp.sum(onehot, axis=0)
    return jnp.dot(onehot, totals, precision=HIGHEST)


def coefficients(record, shifts, per_station, first_time, num_times):
    times_range = first_time + jnp.arange(num_times, dtype=jnp.int32)
    positions = shifts[:, :, None] + times_range[None, None, :]
    values = jnp.take_along_axis(record, positions.reshape(positions.shape[0], -1), axis=1)
    scaled = values.reshape(positions.shape) / per_station[:, None, None]
    return jnp.transpose(scaled, (2, 1, 0)).astype(jnp.bfloat16)


def fourier_parts(length, scale):
    indices = jnp.arange(length, dtype=jnp.int32)
    product = indices[:, None] * indices[None, :] % length
    angles = product.astype(jnp.float32) * (2.0 * math.pi / length)
    return (jnp.cos(angles) * scale, jnp.sin(angles) * scale)


def complex_table(length, forward):
    if forward:
        cosine, sine = fourier_parts(length, 1.0)
        return jnp.stack([jnp.stack([cosine, sine]), jnp.stack([-sine, cosine])])
    cosine, sine = fourier_parts(length, 1.0 / length)
    return jnp.stack([jnp.stack([cosine, -sine]), jnp.stack([sine, cosine])])


def along_rows(piece, table):
    return jnp.einsum("itzny,oikn->otzky", piece, table, precision=HIGHEST)


def along_depth(piece, table):
    return jnp.einsum("itnxy,oikn->otkxy", piece, table, precision=HIGHEST)


def on_device(record, shifts, station_group, weights, psf_real, psf_imag):
    per_station = station_counts(station_group)
    depth_rows = shifts.shape[1]
    lateral_rows = weights.shape[1]
    width_y = weights.shape[2]
    columns = lateral_rows * width_y
    first_time = lax.axis_index("sta") * T_DEV
    coefficient = coefficients(record, shifts, per_station, first_time, T_DEV)
    coefficient = coefficient.reshape(T_DEV * depth_rows, coefficient.shape[2])
    piece = lax.all_gather(weights, "sta", axis=0, tiled=True)
    stack = jnp.dot(
        coefficient, piece.reshape(piece.shape[0], columns), preferred_element_type=jnp.float32
    )
    stack = stack.reshape(T_DEV, depth_rows, lateral_rows, width_y)
    cosine_y, sine_y = fourier_parts(width_y, 1.0)
    spectrum = jnp.einsum(
        "tzxn,okn->otzxk", stack, jnp.stack([cosine_y, -sine_y]), precision=HIGHEST
    )
    row_table = complex_table(NX, True)
    by_rows = along_rows(
        lax.all_to_all(spectrum, "gy", split_axis=4, concat_axis=3, tiled=True), row_table
    )
    depth_table = complex_table(NZ, True)
    by_depth = along_depth(
        lax.all_to_all(by_rows, "gx", split_axis=3, concat_axis=2, tiled=True), depth_table
    )
    power = psf_real * psf_real + psf_imag * psf_imag + NOISE_POWER
    filt_real = (psf_real * by_depth[0] + psf_imag * by_depth[1]) / power
    filt_imag = (psf_real * by_depth[1] - psf_imag * by_depth[0]) / power
    back_depth = along_depth(jnp.stack([filt_real, filt_imag]), complex_table(NZ, False))
    back_table = complex_table(NX, False)
    back_rows = along_rows(
        lax.all_to_all(back_depth, "gx", split_axis=2, concat_axis=3, tiled=True), back_table
    )
    cosine_back, sine_back = fourier_parts(width_y, 1.0 / width_y)
    real_table = jnp.stack([cosine_back, -sine_back])
    return jnp.einsum(
        "itzxk,iyk->tzxy",
        lax.all_to_all(back_rows, "gy", split_axis=3, concat_axis=4, tiled=True),
        real_table,
        precision=HIGHEST,
    )


def solution(mesh):
    in_specs = (
        P(),
        P(None, "gx"),
        P(),
        P("sta", "gy", None),
        P(None, "gx", "gy"),
        P(None, "gx", "gy"),
    )
    out_specs = P("sta", "gx", "gy", None)
    return jax.shard_map(
        on_device, mesh=mesh, in_specs=in_specs, out_specs=out_specs, check_vma=False
    )
```

profile of v0, /device:TPU:0, one launch (start us, length us, event | category | flops | bytes accessed | tf_op | source)
XLA Modules:
  0.0 516.7 jit_solution(10342550417236700609)
XLA Ops:
  7.6 16.6 %gather_fusion = f32[2048]{0:T(1024)S(1)} fusion(f32[128,1024]{1,0:T(8,128)S(1)} %copy-done, s32[2048]{0:T(1024)S(1)} %reshape.275), kind=kCustom, calls=%fused_computation | custom fusion | bytes 32768 | tf_op jit(solution)/shard_map/jit(take_along_axis)/gather | solution.py:25
  24.6 4.1 fusion.27
  28.7 89.3 %all-gather.2.cloned.1.call-done = bf16[128,64,512]{2,1,0:T(8,128)(2,1)} async-done(((bf16[64,64,512]{2,1,0:T(8,128)(2,1)}), bf16[128,64,512]{2,1,0:T(8,128)(2,1)}) %all-gather.2.cloned.1.call-update) | async-done | bytes 8388624 | tf_op jit(solution)/shard_map/all_gather | solution.py:62
  118.0 13.1 %copy.78 = bf16[128,64,512]{0,2,1:T(8,128)(2,1)} copy(bf16[128,64,512]{2,1,0:T(8,128)(2,1)} %all-gather.2.cloned.1.call-done) | data formatting | bytes 16777216 | tf_op jit(solution)/shard_map/reshape | solution.py:64
  131.1 5.8 %fusion = f32[16,64,512]{2,0,1:T(8,128)S(1)} fusion(bf16[128,64,512]{0,2,1:T(8,128)(2,1)} %copy.78, f32[128,16]{1,0:T(8,128)S(1)} %reshape.278, s32[128,16]{1,0:T(8,128)S(1)} %copy.50, f32[128]{0:T(128)S(1)} %convolution_bitcast_fusion.4, s32[]{:T(128)S(6)} %axis_index.15), kind=kOutput, calls=%fused_computation.1 | convolution fusion | flops 134238208 | bytes 10502660 | tf_op jit(solution)/shard_map/dot_general | solution.py:63
  136.9 9.2 %convolution_bitcast_fusion = f32[2,1,16,64,512]{4,3,2,0,1:T(8,128)} fusion(f32[1,512,512]{2,1,0:T(8,128)S(1)} %get-tuple-element.12, f32[1,512,512]{2,1,0:T(8,128)S(1)} %get-tuple-element.11, f32[16,64,512]{2,0,1:T(8,128)S(1)} %fusion), kind=kOutput, calls=%fused_computation.8 | convolution fusion | flops 6442975232 | bytes 8388608 | tf_op jit(solution)/shard_map/tzxn,okn->otzxk/dot_general | solution.py:68
  146.0 9.1 %copy.54 = f32[2,1,16,64,512]{3,2,0,1,4:T(8,128)} copy(f32[2,1,16,64,512]{4,3,2,0,1:T(8,128)} %convolution_bitcast_fusion) | data formatting | bytes 8388608 | tf_op jit(solution)/shard_map/tzxn,okn->otzxk/transpose | solution.py:68
  155.2 19.9 %reshape.303 = f32[4,1,262144]{2,1,0:T(1,128)} reshape(f32[512,1,2,16,64]{4,3,2,1,0:T(8,128)} %bitcast.153) | data formatting | bytes 8388608
  175.1 4.8 all-to-all-start
  182.1 47.0 %all-to-all-done = f32[4,1,262144]{2,1,0:T(1,128)} async-done(((f32[4,1,262144]{2,1,0:T(1,128)}), f32[4,1,262144]{2,1,0:T(1,128)}, u32[]{:S(2)}, u32[]{:S(2)}) %all-to-all-start) | async-done | bytes 4194336 | tf_op jit(solution)/shard_map/all_to_all | solution.py:73
  229.6 15.2 %reduce = f32[4,262144]{1,0:T(4,128)} reduce(f32[4,1,262144]{2,1,0:T(1,128)} %all-to-all-done, f32[]{:T(128)} %broadcast.479), dimensions={1}, to_apply=%all_to_all.44.reduce_sub_computation | reduce | bytes 8388612 | tf_op jit(solution)/shard_map/all_to_all | solution.py:73
  244.8 9.3 %reshape.304 = f32[512,1,2,16,64]{4,3,2,1,0:T(8,128)} reshape(f32[4,262144]{1,0:T(4,128)} %reduce) | data formatting | bytes 8388608
  254.1 6.9 %copy.55 = f32[2,1,16,64,4,128]{5,3,4,0,2,1:T(8,128)} copy(f32[2,1,16,64,4,128]{3,2,0,5,4,1:T(8,128)} %bitcast.154) | data formatting | bytes 8388608 | tf_op jit(solution)/shard_map/all_to_all | solution.py:73
  261.0 8.7 %convolution_bitcast_fusion.3 = f32[2,1,16,256,128]{4,3,2,0,1:T(8,128)S(1)} fusion(f32[2,16,256,128,1]{3,2,0,1,4:T(8,128)} %bitcast.155, f32[1,2,256,256]{3,2,1,0:T(8,128)S(1)} %get-tuple-element.10, f32[1,2,256,256]{3,2,1,0:T(8,128)S(1)} %get-tuple-element.9), kind=kOutput, calls=%fused_computation.12 | convolution fusion | flops 6442713088 | bytes 9437184 | tf_op jit(solution)/shard_map/itzny,oikn->otzky/dot_general | solution.py:46
  269.7 4.4 copy.56
  274.1 6.9 %all-to-all-start.1 = ((f32[2,1,16,256,128]{4,2,0,1,3:T(8,128)}), f32[2,1,16,256,128]{4,2,0,1,3:T(8,128)}, u32[]{:S(2)}, u32[]{:S(2)}) async-start(f32[2,1,16,256,128]{4,2,0,1,3:T(8,128)} %copy.56), calls=%async_computation.1 | async-start | bytes 8388608 | tf_op jit(solution)/shard_map/all_to_all | solution.py:77
  282.0 1.1 broadcast_multiply_fusion.1
  283.1 53.2 %all-to-all-done.1 = f32[2,1,16,256,128]{4,2,0,1,3:T(8,128)} async-done(((f32[2,1,16,256,128]{4,2,0,1,3:T(8,128)}), f32[2,1,16,256,128]{4,2,0,1,3:T(8,128)}, u32[]{:S(2)}, u32[]{:S(2)}) %all-to-all-start.1) | async-done | bytes 4194336 | tf_op jit(solution)/shard_map/all_to_all | solution.py:77
  336.3 2.7 copy.57
  339.1 7.1 %convolution_bitcast_fusion.2 = f32[2,256,16,128]{3,1,2,0:T(8,128)S(1)} fusion(f32[2,256,16,128,1]{3,1,0,2,4:T(8,128)S(1)} %bitcast.157, f32[1,2,256,256]{3,2,1,0:T(8,128)S(1)} %get-tuple-element.10, f32[1,2,256,256]{3,2,1,0:T(8,128)S(1)} %get-tuple-element.9), kind=kOutput, calls=%fused_computation.11 | convolution fusion | flops 6442713088 | bytes 9437184 | tf_op jit(solution)/shard_map/itnxy,oikn->otkxy/dot_general | solution.py:50
  346.2 1.5 fusion.13
  347.7 7.3 %fusion.5 = f32[2,1,256,16,128]{4,2,3,0,1:T(8,128)S(1)} fusion(f32[1,2,256,256]{3,2,1,0:T(8,128)S(1)} %get-tuple-element.8, f32[1,2,256,256]{3,2,1,0:T(8,128)S(1)} %get-tuple-element.7, f32[1,1,256,16,128]{4,2,3,1,0:T(8,128)S(1)} %get-tuple-element.6, f32[1,1,256,16,128]{4,2,3,1,0:T(8,128)S(1)} %get-tuple-element.5), kind=kOutput, calls=%fused_computation.9 | convolution fusion | flops 6443761664 | bytes 9437184 | tf_op jit(solution)/shard_map/itnxy,oikn->otkxy/dot_general | solution.py:50
  355.0 2.4 copy.64
  357.5 64.3 %all_to_all.60 = f32[2,1,256,16,128]{4,3,0,1,2:T(8,128)S(1)} all-to-all(f32[2,1,256,16,128]{4,3,0,1,2:T(8,128)S(1)} %copy.64), channel_id=1, replica_groups=mesh['sta'=2,'gx'=16,'gy'=4] {'gx'}, dimensions={2} | all-to-all | bytes 8388608 | tf_op jit(solution)/shard_map/all_to_all | solution.py:85
  422.3 6.9 %convolution_bitcast_fusion.1 = f32[2,1,16,256,128]{4,3,2,0,1:T(8,128)S(1)} fusion(f32[2,16,256,128,1]{3,2,0,1,4:T(8,128)S(1)} %bitcast.156, f32[1,2,256,256]{3,2,1,0:T(8,128)S(1)} %get-tuple-element.8, f32[1,2,256,256]{3,2,1,0:T(8,128)S(1)} %get-tuple-element.7), kind=kOutput, calls=%fused_computation.10 | convolution fusion | flops 6442713088 | bytes 9437184 | tf_op jit(solution)/shard_map/itzny,oikn->otzky/dot_general | solution.py:46
  429.2 4.4 copy.66
  433.6 5.1 all-to-all-start.3
  438.7 4.2 multiply_negate_fusion
  442.8 44.5 %all-to-all-done.3 = f32[2,1,16,256,128]{4,2,0,1,3:T(8,128)} async-done(((f32[2,1,16,256,128]{4,2,0,1,3:T(8,128)}), f32[2,1,16,256,128]{4,2,0,1,3:T(8,128)}, u32[]{:S(2)}, u32[]{:S(2)}) %all-to-all-start.3) | async-done | bytes 4194336 | tf_op jit(solution)/shard_map/all_to_all | solution.py:91
  487.3 6.9 %copy.94 = f32[2,1,16,4,64,128]{5,3,4,0,2,1:T(4,128)} copy(f32[2,1,16,4,64,128]{5,2,0,4,3,1:T(8,128)} %bitcast.57) | data formatting | bytes 8388608 | tf_op jit(solution)/shard_map/all_to_all | solution.py:91
  494.2 5.5 %reshape.274 = f32[2,16,64,512]{3,2,0,1:T(8,128)} reshape(f32[2,1,16,64,4,128]{5,4,3,0,2,1:T(4,128)} %bitcast.159) | data formatting | bytes 8388608 | tf_op jit(solution)/shard_map/reshape.27
  499.7 9.9 %fusion.19 = f32[1,16,64,512]{3,2,1,0:T(8,128)} fusion(f32[2,16,64,512]{3,2,0,1:T(8,128)} %reshape.274, f32[1,512,512]{2,1,0:T(8,128)S(1)} %get-tuple-element.17, f32[1,512,512]{2,1,0:T(8,128)S(1)} %get-tuple-element.18), kind=kOutput, calls=%fused_computation.33 | convolution fusion | flops 6442975232 | bytes 8388608 | tf_op jit(solution)/shard_map/itzxk,iyk->tzxy/dot_general | solution.py:89
  (27 shorter events, 5.6 us)
Async XLA Ops:
  6.5 1.1 copy-start
  6.5 0.8 copy-start.4
  6.5 111.5 %all-gather.2.cloned.1.call-start = ((), (), s32[]{:S(2)}) async-start(), calls=%async_computation.4 | async-start | bytes 12582912 | tf_op jit(solution)/shard_map/all_gather | solution.py:62
  7.6 16.7 %copy-start.5 = (s32[128]{0:T(128)S(1)}, s32[128]{0:T(128)}, u32[]{:S(2)}) copy-start(s32[128]{0:T(128)} %param.8) | copy-start | bytes 1540
  175.1 54.0 %all-to-all-start = ((f32[4,1,262144]{2,1,0:T(1,128)}), f32[4,1,262144]{2,1,0:T(1,128)}, u32[]{:S(2)}, u32[]{:S(2)}) async-start(f32[4,1,262144]{2,1,0:T(1,128)} %reshape.303), calls=%async_computation | async-start | bytes 8388608 | tf_op jit(solution)/shard_map/all_to_all | solution.py:73
  274.1 62.2 %all-to-all-start.1 = ((f32[2,1,16,256,128]{4,2,0,1,3:T(8,128)}), f32[2,1,16,256,128]{4,2,0,1,3:T(8,128)}, u32[]{:S(2)}, u32[]{:S(2)}) async-start(f32[2,1,16,256,128]{4,2,0,1,3:T(8,128)} %copy.56), calls=%async_computation.1 | async-start | bytes 8388608 | tf_op jit(solution)/shard_map/all_to_all | solution.py:77
  339.0 7.2 %copy-start.2 = (f32[256,16,128]{2,1,0:T(8,128)S(1)}, f32[256,16,128]{2,1,0:T(8,128)}, u32[]{:S(2)}) copy-start(f32[256,16,128]{2,1,0:T(8,128)} %param.11) | copy-start | bytes 6291460
  339.0 7.2 %copy-start.3 = (f32[256,16,128]{2,1,0:T(8,128)S(1)}, f32[256,16,128]{2,1,0:T(8,128)}, u32[]{:S(2)}) copy-start(f32[256,16,128]{2,1,0:T(8,128)} %param.10) | copy-start | bytes 6291460
  433.6 53.7 %all-to-all-start.3 = ((f32[2,1,16,256,128]{4,2,0,1,3:T(8,128)}), f32[2,1,16,256,128]{4,2,0,1,3:T(8,128)}, u32[]{:S(2)}, u32[]{:S(2)}) async-start(f32[2,1,16,256,128]{4,2,0,1,3:T(8,128)} %copy.66), calls=%async_computation.3 | async-start | bytes 8388608 | tf_op jit(solution)/shard_map/all_to_all | solution.py:91
  499.7 9.9 %copy-start.1 = (f32[128,1024]{1,0:T(8,128)S(1)}, f32[128,1024]{1,0:T(8,128)}, u32[]{:S(2)}) copy-start(f32[128,1024]{1,0:T(8,128)} %param.6) | copy-start | bytes 1572868
Sparse Core Ops, SparseCore 0:
  9.0 108.9 all-gather.1
where the time goes:
time: 526 us; the launch traced here: 517 us
  waiting for transfers between devices  235 us (45%)
  local copies, waits for them, and re-layouts  103 us (20%)
  blocking collectives  64.3 us (12%)
  matrix products  55 us (10%)
  other arithmetic  29.4 us (6%)
  starting transfers between devices  16.8 us (3%)
  between operations  13.8 us (3%)
    all_gather x1, waiting for transfers between devices, on_device(): piece = lax.all_gather(weights, 'sta', axis=0, tiled=True)  89.3 us
    all_to_all x1, blocking collectives, on_device(): lax.all_to_all(back_depth, 'gx', split_axis=2, concat_axis=3, tiled=True)  64.3 us
    all_to_all x1, waiting for transfers between devices, on_device(): lax.all_to_all(by_rows, 'gx', split_axis=3, concat_axis=2, tiled=True)  53.2 us
    all_to_all x1, waiting for transfers between devices, on_device(): lax.all_to_all(spectrum, 'gy', split_axis=4, concat_axis=3, tiled=True)  47 us
    all_to_all x1, waiting for transfers between devices, on_device(): lax.all_to_all(back_rows, 'gy', split_axis=3, concat_axis=4, tiled=True)  44.5 us
    unnamed x15, local copies, waits for them, and re-layouts  29.4 us
    gather x3, local copies, waits for them, and re-layouts, coefficients(): jnp.take_along_axis(record, positions.reshape(positions.shape[0], -1), ax...  16.8 us
    dot_general x2, matrix products, along_rows(): return jnp.einsum('itzny,oikn->otzky', piece, table, precision=HIGHEST)  15.6 us
  transfers between devices with their start and end apart: 4, of which 4 were waited for; matrix products, arithmetic and copies ran while one was open for 6% of the time, Pallas kernels for 0%

commit v1 on v0

--- a/solution.py
+++ b/solution.py
@@ -10,6 +10,29 @@
 GROUPS = 8
 NOISE_POWER = 0.25
 HIGHEST = lax.Precision.HIGHEST
+
+
+def cut_along(array, dim, size):
+    lengths = array.shape
+    parts = array.reshape(*lengths[:dim], size, lengths[dim] // size, *lengths[dim + 1 :])
+    return jnp.moveaxis(parts, dim, 0)
+
+
+def joined_along(parts, dim):
+    parts = jnp.moveaxis(parts, 0, dim)
+    shape = parts.shape
+    return parts.reshape(*shape[:dim], shape[dim] * shape[dim + 1], *shape[dim + 2 :])
+
+
+def pairwise_exchange(value, axis, split_dim, concat_dim):
+    devices, mine = (lax.axis_size(axis), lax.axis_index(axis))
+    parts = cut_along(value, split_dim, devices)
+    finished = [parts[mine]]
+    for step in range(1, devices):
+        sent = parts[mine ^ step]
+        finished.append(lax.ppermute(sent, axis, [(i, i ^ step) for i in range(devices)]))
+    parts = jnp.stack(finished)[mine ^ jnp.arange(devices)]
+    return joined_along(parts, concat_dim)
 
 
 def station_counts(station_group):
@@ -69,9 +92,7 @@
         "tzxn,okn->otzxk", stack, jnp.stack([cosine_y, -sine_y]), precision=HIGHEST
     )
     row_table = complex_table(NX, True)
-    by_rows = along_rows(
-        lax.all_to_all(spectrum, "gy", split_axis=4, concat_axis=3, tiled=True), row_table
-    )
+    by_rows = along_rows(pairwise_exchange(spectrum, "gy", 4, 3), row_table)
     depth_table = complex_table(NZ, True)
     by_depth = along_depth(
         lax.all_to_all(by_rows, "gx", split_axis=3, concat_axis=2, tiled=True), depth_table

time: 526 us -> 496 us (0.943)
  other arithmetic: 29.4 us -> 16.4 us
  local copies, waits for them, and re-layouts: 103 us -> 92.8 us
    all_to_all x1 -> x0, waiting for transfers between devices: 47 us -> none  [on_device(): lax.all_to_all(spectrum, 'gy', split_axis=4, concat_axis=3, tiled=True)]
    ppermute x0 -> x3, waiting for transfers between devices: none -> 43 us  [pairwise_exchange(): lax.ppermute(sent, axis, [(i, i ^ step) for i in range(devices)])]
    unnamed x15 -> x13, local copies, waits for them, and re-layouts: 29.4 us -> 0.22 us
    reshape x0 -> x1, local copies, waits for them, and re-layouts: none -> 17.2 us  [cut_along(): array.reshape(*lengths[:dim], size, lengths[dim] // size, *lengths[dim +...]
    all_to_all x1 -> x0, other arithmetic: 15.2 us -> none  [on_device(): lax.all_to_all(spectrum, 'gy', split_axis=4, concat_axis=3, tiled=True)]
    another operation x1 -> x2, local copies, waits for them, and re-layouts: 5.49 us -> 16.2 us
    all_to_all x2 -> x0, local copies, waits for them, and re-layouts: 7.36 us -> none  [on_device(): lax.all_to_all(spectrum, 'gy', split_axis=4, concat_axis=3, tiled=True)]
    transpose x1, local copies, waits for them, and re-layouts: 9.13 us -> 2.49 us  [joined_along(): parts = jnp.moveaxis(parts, 0, dim)]
  transfers between devices with their start and end apart: 4 -> 6, of which waited for: 4 -> 5; matrix products, arithmetic and copies ran while one was open for 6% -> 6% of each run, Pallas kernels for 0% -> 0%
where the time goes in v1:
time: 496 us; the launch traced here: 487 us
  waiting for transfers between devices  231 us (47%)
  local copies, waits for them, and re-layouts  92.8 us (19%)
  blocking collectives  64.4 us (13%)
  matrix products  52.9 us (11%)
  other arithmetic  16.4 us (3%)
  starting transfers between devices  16 us (3%)
  between operations  14.1 us (3%)
    all_gather x1, waiting for transfers between devices, on_device(): piece = lax.all_gather(weights, 'sta', axis=0, tiled=True)  89.3 us
    all_to_all x1, blocking collectives, on_device(): lax.all_to_all(back_depth, 'gx', split_axis=2, concat_axis=3, tiled=True)  64.4 us
    all_to_all x1, waiting for transfers between devices, on_device(): lax.all_to_all(by_rows, 'gx', split_axis=3, concat_axis=2, tiled=True)  53.4 us
    all_to_all x1, waiting for transfers between devices, on_device(): lax.all_to_all(back_rows, 'gy', split_axis=3, concat_axis=4, tiled=True)  44.5 us
    ppermute x3, waiting for transfers between devices, pairwise_exchange(): lax.ppermute(sent, axis, [(i, i ^ step) for i in range(devices)])  43 us
    reshape x1, local copies, waits for them, and re-layouts, cut_along(): array.reshape(*lengths[:dim], size, lengths[dim] // size, *lengths[dim +...  17.2 us
    gather x3, local copies, waits for them, and re-layouts, coefficients(): jnp.take_along_axis(record, positions.reshape(positions.shape[0], -1), ax...  16.8 us
    another operation x2, local copies, waits for them, and re-layouts  16.2 us
  transfers between devices with their start and end apart: 6, of which 5 were waited for; matrix products, arithmetic and copies ran while one was open for 6% of the time, Pallas kernels for 0%

profile of v1, /device:TPU:0, one launch (start us, length us, event | category | flops | bytes accessed | tf_op | source)
XLA Modules:
  0.0 487.3 jit_solution(2113954405603891690)
XLA Ops:
  7.6 16.6 %gather_fusion.1 = f32[2048]{0:T(1024)S(1)} fusion(f32[128,1024]{1,0:T(8,128)S(1)} %copy-done, s32[2048]{0:T(1024)S(1)} %reshape.313), kind=kCustom, calls=%fused_computation.1 | custom fusion | bytes 32768 | tf_op jit(solution)/shard_map/jit(take_along_axis)/gather | solution.py:48
  24.6 4.1 fusion.33
  28.7 89.3 %all-gather.2.cloned.1.call-done = bf16[128,64,512]{2,1,0:T(8,128)(2,1)} async-done(((bf16[64,64,512]{2,1,0:T(8,128)(2,1)}), bf16[128,64,512]{2,1,0:T(8,128)(2,1)}) %all-gather.2.cloned.1.call-update) | async-done | bytes 8388624 | tf_op jit(solution)/shard_map/all_gather | solution.py:85
  118.0 13.0 %copy.92 = bf16[128,64,512]{0,2,1:T(8,128)(2,1)} copy(bf16[128,64,512]{2,1,0:T(8,128)(2,1)} %all-gather.2.cloned.1.call-done) | data formatting | bytes 16777216 | tf_op jit(solution)/shard_map/reshape | solution.py:87
  131.0 5.8 %fusion = f32[16,64,512]{2,0,1:T(8,128)S(1)} fusion(bf16[128,64,512]{0,2,1:T(8,128)(2,1)} %copy.92, f32[128,16]{1,0:T(8,128)S(1)} %reshape.316, s32[128,16]{1,0:T(8,128)S(1)} %copy.64, f32[128]{0:T(128)S(1)} %convolution_bitcast_fusion.3, s32[]{:T(128)S(6)} %axis_index.23), kind=kOutput, calls=%fused_computation.2 | convolution fusion | flops 134238208 | bytes 10502660 | tf_op jit(solution)/shard_map/dot_general | solution.py:86
  136.8 9.2 %convolution_bitcast_fusion = f32[2,1,16,64,512]{4,3,2,0,1:T(8,128)} fusion(f32[1,512,512]{2,1,0:T(8,128)S(1)} %get-tuple-element.16, f32[1,512,512]{2,1,0:T(8,128)S(1)} %get-tuple-element.15, f32[16,64,512]{2,0,1:T(8,128)S(1)} %fusion), kind=kOutput, calls=%fused_computation.13 | convolution fusion | flops 6442975232 | bytes 8388608 | tf_op jit(solution)/shard_map/tzxn,okn->otzxk/dot_general | solution.py:91
  145.9 17.2 %reshape.297 = f32[2,1,16,64,4,128]{5,4,3,2,0,1:T(4,128)} reshape(f32[2,1,16,64,512]{4,3,2,0,1:T(8,128)} %convolution_bitcast_fusion) | data formatting | bytes 8388608 | tf_op jit(solution)/shard_map/reshape | solution.py:17
  163.1 10.8 %constant_dynamic-slice_fusion.3 = (f32[2,1,16,64,1,128]{5,4,3,2,0,1:T(1,128)S(1)}, f32[2,1,16,64,1,128]{5,4,3,2,0,1:T(1,128)S(1)}, f32[2,1,16,64,1,128]{5,4,3,2,0,1:T(1,128)S(1)}, f32[2,1,16,64,1,128]{5,4,3,2,0,1:T(1,128)S(1)}) fusion(f32[2,1,16,64,4,128]{5,4,3,2,0,1:T(4,128)} %reshape.297, s32[]{:T(128)S(6)} %select_n.128, s32[]{:T(128)S(6)} %select_n.131, ...), kind=kLoop, calls=%fused_computation.92 | loop fusion | bytes 8388624 | tf_op jit(solution)/shard_map/dynamic-slice
  173.9 2.8 collective-permute-start.2
  180.2 42.4 %collective-permute-done.2 = f32[2,1,16,64,128]{4,3,2,0,1:T(8,128)S(1)} collective-permute-done((f32[2,1,16,64,128]{4,3,2,0,1:T(8,128)S(1)}, f32[2,1,16,64,128]{4,3,2,0,1:T(8,128)S(1)}, u32[]{:S(2)}, u32[]{:S(2)}) %collective-permute-start.2) | collective-permute-done | bytes 1048608 | tf_op jit(solution)/shard_map/ppermute | solution.py:33
  223.2 2.3 maximum_bitcast_fusion
  225.5 5.0 %gather_fusion = f32[4,2,16,64,128]{4,3,2,1,0:T(8,128)} fusion(f32[4,2,16,64,128]{4,3,2,1,0:T(8,128)} %maximum_bitcast_fusion, s32[1024]{0:T(1024)S(1)} %pad_clamp_fusion), kind=kCustom, calls=%fused_computation | custom fusion | bytes 8388624 | tf_op jit(solution)/shard_map/gather | solution.py:34
  230.5 2.5 copy.68
  232.9 6.8 %fusion.8 = f32[2,1,16,256,128]{4,3,2,0,1:T(8,128)S(1)} fusion(f32[2,16,256,128]{3,2,1,0:T(8,128)S(1)} %bitcast.169, f32[1,2,256,256]{3,2,1,0:T(8,128)S(1)} %get-tuple-element.14, f32[1,2,256,256]{3,2,1,0:T(8,128)S(1)} %get-tuple-element.13), kind=kOutput, calls=%fused_computation.14 | convolution fusion | flops 6442713088 | bytes 9437184 | tf_op jit(solution)/shard_map/itzny,oikn->otzky/dot_general | solution.py:69
  239.8 4.8 copy.70
  244.6 6.7 %all-to-all-start = ((f32[2,1,16,256,128]{4,2,0,1,3:T(8,128)}), f32[2,1,16,256,128]{4,2,0,1,3:T(8,128)}, u32[]{:S(2)}, u32[]{:S(2)}) async-start(f32[2,1,16,256,128]{4,2,0,1,3:T(8,128)} %copy.70), calls=%async_computation | async-start | bytes 8388608 | tf_op jit(solution)/shard_map/all_to_all | solution.py:98
  252.3 1.1 broadcast_multiply_fusion.1
  253.5 53.4 %all-to-all-done = f32[2,1,16,256,128]{4,2,0,1,3:T(8,128)} async-done(((f32[2,1,16,256,128]{4,2,0,1,3:T(8,128)}), f32[2,1,16,256,128]{4,2,0,1,3:T(8,128)}, u32[]{:S(2)}, u32[]{:S(2)}) %all-to-all-start) | async-done | bytes 4194336 | tf_op jit(solution)/shard_map/all_to_all | solution.py:98
  306.8 2.7 copy.71
  309.6 7.1 %convolution_bitcast_fusion.2 = f32[2,256,16,128]{3,1,2,0:T(8,128)S(1)} fusion(f32[2,256,16,128,1]{3,1,0,2,4:T(8,128)S(1)} %bitcast.170, f32[1,2,256,256]{3,2,1,0:T(8,128)S(1)} %get-tuple-element.14, f32[1,2,256,256]{3,2,1,0:T(8,128)S(1)} %get-tuple-element.13), kind=kOutput, calls=%fused_computation.17 | convolution fusion | flops 6442713088 | bytes 9437184 | tf_op jit(solution)/shard_map/itnxy,oikn->otkxy/dot_general | solution.py:73
  316.8 1.5 fusion.19
  318.3 7.1 %fusion.11 = f32[2,1,256,16,128]{4,2,3,0,1:T(8,128)S(1)} fusion(f32[1,2,256,256]{3,2,1,0:T(8,128)S(1)} %get-tuple-element.12, f32[1,2,256,256]{3,2,1,0:T(8,128)S(1)} %get-tuple-element.11, f32[1,1,256,16,128]{4,2,3,1,0:T(8,128)S(1)} %get-tuple-element.6, f32[1,1,256,16,128]{4,2,3,1,0:T(8,128)S(1)} %get-tuple-element.5), kind=kOutput, calls=%fused_computation.15 | convolution fusion | flops 6443761664 | bytes 9437184 | tf_op jit(solution)/shard_map/itnxy,oikn->otkxy/dot_general | solution.py:73
  325.3 2.4 copy.78
  327.8 64.4 %all_to_all.45 = f32[2,1,256,16,128]{4,3,0,1,2:T(8,128)S(1)} all-to-all(f32[2,1,256,16,128]{4,3,0,1,2:T(8,128)S(1)} %copy.78), channel_id=1, replica_groups=mesh['sta'=2,'gx'=16,'gy'=4] {'gx'}, dimensions={2} | all-to-all | bytes 8388608 | tf_op jit(solution)/shard_map/all_to_all | solution.py:106
  392.7 6.9 %convolution_bitcast_fusion.1 = f32[2,1,16,256,128]{4,3,2,0,1:T(8,128)S(1)} fusion(f32[2,16,256,128,1]{3,2,0,1,4:T(8,128)S(1)} %bitcast.168, f32[1,2,256,256]{3,2,1,0:T(8,128)S(1)} %get-tuple-element.12, f32[1,2,256,256]{3,2,1,0:T(8,128)S(1)} %get-tuple-element.11), kind=kOutput, calls=%fused_computation.16 | convolution fusion | flops 6442713088 | bytes 9437184 | tf_op jit(solution)/shard_map/itzny,oikn->otzky/dot_general | solution.py:69
  399.5 4.4 copy.80
  404.0 5.1 %all-to-all-start.2 = ((f32[2,1,16,256,128]{4,2,0,1,3:T(8,128)}), f32[2,1,16,256,128]{4,2,0,1,3:T(8,128)}, u32[]{:S(2)}, u32[]{:S(2)}) async-start(f32[2,1,16,256,128]{4,2,0,1,3:T(8,128)} %copy.80), calls=%async_computation.2 | async-start | bytes 8388608 | tf_op jit(solution)/shard_map/all_to_all | solution.py:112
  409.1 4.2 multiply_negate_fusion
  413.2 44.5 %all-to-all-done.2 = f32[2,1,16,256,128]{4,2,0,1,3:T(8,128)} async-done(((f32[2,1,16,256,128]{4,2,0,1,3:T(8,128)}), f32[2,1,16,256,128]{4,2,0,1,3:T(8,128)}, u32[]{:S(2)}, u32[]{:S(2)}) %all-to-all-start.2) | async-done | bytes 4194336 | tf_op jit(solution)/shard_map/all_to_all | solution.py:112
  457.7 6.9 %copy.114 = f32[2,1,16,4,64,128]{5,3,4,0,2,1:T(4,128)} copy(f32[2,1,16,4,64,128]{5,2,0,4,3,1:T(8,128)} %bitcast.66) | data formatting | bytes 8388608 | tf_op jit(solution)/shard_map/all_to_all | solution.py:112
  464.6 5.5 %reshape.302 = f32[2,16,64,512]{3,2,0,1:T(8,128)} reshape(f32[2,1,16,64,4,128]{5,4,3,0,2,1:T(4,128)} %bitcast.173) | data formatting | bytes 8388608 | tf_op jit(solution)/shard_map/reshape.29
  470.1 9.9 %fusion.25 = f32[1,16,64,512]{3,2,1,0:T(8,128)} fusion(f32[2,16,64,512]{3,2,0,1:T(8,128)} %reshape.302, f32[1,512,512]{2,1,0:T(8,128)S(1)} %get-tuple-element.21, f32[1,512,512]{2,1,0:T(8,128)S(1)} %get-tuple-element.22), kind=kOutput, calls=%fused_computation.38 | convolution fusion | flops 6442975232 | bytes 8388608 | tf_op jit(solution)/shard_map/itzxk,iyk->tzxy/dot_general | solution.py:110
  (32 shorter events, 7.1 us)
Async XLA Ops:
  6.5 1.1 copy-start
  6.5 0.8 copy-start.4
  6.5 111.5 %all-gather.2.cloned.1.call-start = ((), (), s32[]{:S(2)}) async-start(), calls=%async_computation.3 | async-start | bytes 12582912 | tf_op jit(solution)/shard_map/all_gather | solution.py:85
  7.6 16.8 %copy-start.5 = (s32[128]{0:T(128)S(1)}, s32[128]{0:T(128)}, u32[]{:S(2)}) copy-start(s32[128]{0:T(128)} %param.8) | copy-start | bytes 1540
  173.9 48.7 %collective-permute-start.2 = (f32[2,1,16,64,128]{4,3,2,0,1:T(8,128)S(1)}, f32[2,1,16,64,128]{4,3,2,0,1:T(8,128)S(1)}, u32[]{:S(2)}, u32[]{:S(2)}) collective-permute-start(f32[2,1,16,64,128]{4,3,2,0,1:T(8,128)S(1)} %bitcast.177), channel_id=1, source_target_pairs={{0,3},{1,2},{2,1},{3,0},{4,7},{5,6},{6,5},{7,4},{8,11},{9,10},{10,... | collective-permute-start | bytes 3145736 | tf_op jit(solution)/shard_map/ppermute | solution.py:33
  176.7 45.8 %collective-permute-start.1 = (f32[2,1,16,64,128]{4,3,2,0,1:T(8,128)S(1)}, f32[2,1,16,64,128]{4,3,2,0,1:T(8,128)S(1)}, u32[]{:S(2)}, u32[]{:S(2)}) collective-permute-start(f32[2,1,16,64,128]{4,3,2,0,1:T(8,128)S(1)} %bitcast.176), channel_id=1, source_target_pairs={{0,2},{1,3},{2,0},{3,1},{4,6},{5,7},{6,4},{7,5},{8,10},{9,11},{10,... | collective-permute-start | bytes 3145736 | tf_op jit(solution)/shard_map/ppermute | solution.py:33
  177.6 45.6 %collective-permute-start = (f32[2,1,16,64,128]{4,3,2,0,1:T(8,128)S(1)}, f32[2,1,16,64,128]{4,3,2,0,1:T(8,128)S(1)}, u32[]{:S(2)}, u32[]{:S(2)}) collective-permute-start(f32[2,1,16,64,128]{4,3,2,0,1:T(8,128)S(1)} %bitcast.175), channel_id=1, source_target_pairs={{0,1},{1,0},{2,3},{3,2},{4,5},{5,4},{6,7},{7,6},{8,9},{9,8},{10,11... | collective-permute-start | bytes 3145736 | tf_op jit(solution)/shard_map/ppermute | solution.py:33
  244.6 62.2 %all-to-all-start = ((f32[2,1,16,256,128]{4,2,0,1,3:T(8,128)}), f32[2,1,16,256,128]{4,2,0,1,3:T(8,128)}, u32[]{:S(2)}, u32[]{:S(2)}) async-start(f32[2,1,16,256,128]{4,2,0,1,3:T(8,128)} %copy.70), calls=%async_computation | async-start | bytes 8388608 | tf_op jit(solution)/shard_map/all_to_all | solution.py:98
  309.6 7.2 %copy-start.2 = (f32[256,16,128]{2,1,0:T(8,128)S(1)}, f32[256,16,128]{2,1,0:T(8,128)}, u32[]{:S(2)}) copy-start(f32[256,16,128]{2,1,0:T(8,128)} %param.11) | copy-start | bytes 6291460
  309.6 7.2 %copy-start.3 = (f32[256,16,128]{2,1,0:T(8,128)S(1)}, f32[256,16,128]{2,1,0:T(8,128)}, u32[]{:S(2)}) copy-start(f32[256,16,128]{2,1,0:T(8,128)} %param.10) | copy-start | bytes 6291460
  404.0 53.7 %all-to-all-start.2 = ((f32[2,1,16,256,128]{4,2,0,1,3:T(8,128)}), f32[2,1,16,256,128]{4,2,0,1,3:T(8,128)}, u32[]{:S(2)}, u32[]{:S(2)}) async-start(f32[2,1,16,256,128]{4,2,0,1,3:T(8,128)} %copy.80), calls=%async_computation.2 | async-start | bytes 8388608 | tf_op jit(solution)/shard_map/all_to_all | solution.py:112
  470.1 9.9 %copy-start.1 = (f32[128,1024]{1,0:T(8,128)S(1)}, f32[128,1024]{1,0:T(8,128)}, u32[]{:S(2)}) copy-start(f32[128,1024]{1,0:T(8,128)} %param.6) | copy-start | bytes 1572868
Sparse Core Ops, SparseCore 0:
  9.0 108.9 all-gather.1
